TPU v7x, 512 devices: a whole 4x8x8 slice. The times are simulated.
512 devices in a mesh: rows: 128 (over y_hi, x, z), rep: 4 (over y_lo, core).
Axes of the slice: x: 4, y: 8 (y_hi: 4, y_lo: 2; y = y_hi * 2 + y_lo), z: 8, core: 2. Of those that a mesh axis runs over, the one named last changes fastest.
Arguments:
- features: bfloat16 [65536, 256], P(('rows', 'rep')), may hold values from -6 to 6
- weight: bfloat16 [256, 256], replicated, may hold values from -0.375 to 0.375
- bias_terms: float32 [256], replicated, may hold values from -3 to 3
- tile_data: bfloat16 [128, 4, 8, 128, 128], P('rows'), may hold values from -0.1875 to 0.1875
- tile_row: int32 [128, 4, 8], P('rows'), may hold values from 0 to 3
- tile_col: int32 [128, 4, 8], P('rows'), may hold values from 0 to 127
- tile_count: int32 [128, 4], P('rows'), may hold values from 1 to 8, as said below
- grad_out: bfloat16 [65536, 256], P(('rows', 'rep')), may hold values from -6 to 6
Outputs:
- layer_out: bfloat16 [65536, 256], P(('rows', 'rep'))
- weight_grad: float32 [256, 256], replicated
- bias_grad: float32 [256], replicated
Inputs may be any that keep to these rules, and one draw needn't show every extreme that they name: `tile_count`: some group's stripe has all 8 slots live in every draw.
All inputs are finite; a program needn't handle non-finite values.
Results may differ from a plain program's by a relative error of at most 0.015.
Values may be sent and summed in bfloat16 or wider, within the bound.
No kernel may reach another device: no remote copies, remote signals or barrier semaphores. Data moves between devices by JAX's collectives and lax.ppermute only.
A program may use at most 64 MiB of HBM per device.

v0:
```python
import jax
import jax.numpy as jnp
from jax import lax
from jax.sharding import PartitionSpec as P


def slots_wide(tile_set, row_set, col_set, live_set, blocks, row_count):
    picked = jnp.take(blocks, col_set, axis=0)
    product = jnp.einsum("tij,tjf->tif", tile_set, picked, preferred_element_type=jnp.float32)
    local_ids = jnp.arange(row_count, dtype=jnp.int32)
    select = ((row_set[None, :] == local_ids[:, None]) & live_set[None, :]).astype(jnp.float32)
    return jnp.einsum("bt,tif->bif", select, product)


def propagate(tile_set, row_set, col_set, count_set, blocks, row_count, slot_fn):
    stripes, capacity = row_set.shape
    block_size = tile_set.shape[-1]
    slot_ids = jnp.arange(capacity, dtype=jnp.int32)
    live_set = slot_ids[None, :] < count_set[:, None]
    accumulated = slot_fn(
        tile_set.reshape(-1, block_size, block_size),
        row_set.reshape(-1),
        col_set.reshape(-1),
        live_set.reshape(-1),
        blocks,
        row_count,
    )
    return accumulated


def shards(features, weight, bias_terms, tile_data, tile_row, tile_col, tile_count, grad_out):
    block_size = tile_data.shape[-1]
    feature_width = features.shape[1]
    row_count = lax.axis_size("rep")
    rep_index = lax.axis_index("rep")
    own_tiles = lax.dynamic_slice_in_dim(tile_data[0], rep_index, 1, 0)
    own_rows = lax.dynamic_slice_in_dim(tile_row[0], rep_index, 1, 0)
    own_cols = lax.dynamic_slice_in_dim(tile_col[0], rep_index, 1, 0)
    own_count = lax.dynamic_slice_in_dim(tile_count[0], rep_index, 1, 0)
    stripe_nodes = lax.all_gather(features, "rows", axis=0, tiled=True)
    blocks = stripe_nodes.reshape(-1, block_size, feature_width)
    partial_value = propagate(
        own_tiles, own_rows, own_cols, own_count, blocks, row_count, slots_wide
    )
    partial_value = partial_value.reshape(row_count * block_size, feature_width)
    propagated = lax.psum_scatter(partial_value, "rep", scatter_dimension=0, tiled=True).astype(
        jnp.bfloat16
    )
    preact = jnp.dot(propagated, weight, preferred_element_type=jnp.float32) + bias_terms
    sigma = jax.nn.sigmoid(preact)
    layer_out = (preact * sigma).astype(jnp.bfloat16)
    slope = sigma * (1.0 + preact * (1.0 - sigma))
    grad_pre = (grad_out.astype(jnp.float32) * slope).astype(jnp.bfloat16)
    weight_term = lax.dot_general(
        propagated, grad_pre, (((0,), (0,)), ((), ())), preferred_element_type=jnp.float32
    )
    bias_term = jnp.sum(grad_pre.astype(jnp.float32), axis=0)
    weight_grad, bias_grad = lax.psum((weight_term, bias_term), ("rows", "rep"))
    return (layer_out, weight_grad, bias_grad)


def solution(mesh):
    placed = (
        P(("rows", "rep"), None),
        P(),
        P(),
        P("rows", None, None, None, None),
        P("rows", None, None),
        P("rows", None, None),
        P("rows", None),
        P(("rows", "rep"), None),
    )
    return jax.shard_map(
        shards,
        mesh=mesh,
        in_specs=placed,
        out_specs=(P(("rows", "rep"), None), P(), P()),
        check_vma=False,
    )
```

profile of v0, /device:TPU:23, one launch (start us, length us, event | category | flops | bytes accessed | tf_op | source)
XLA Modules:
  0.0 482.8 jit_solution(15143895187925583589)
XLA Ops:
  7.2 0.0 copy-start
  7.2 0.0 all-gather.2.cloned.1.call-start
  7.2 0.7 all-gather.2.cloned.1.call-update
  7.9 0.0 reduce-scatter.2.cloned.1.call-start
  8.0 1.2 constant_dynamic-slice_fusion.1
  9.2 0.7 fusion.18
  9.9 0.7 compare_and_fusion
  10.6 0.6 iota_compare_fusion.1
  11.2 0.7 fusion.17
  11.9 154.5 %all-gather.2.cloned.1.call-done = bf16[16384,256]{1,0:T(8,128)(2,1)} async-done(((bf16[128,256]{1,0:T(8,128)(2,1)}), bf16[16384,256]{1,0:T(8,128)(2,1)}) %all-gather.2.cloned.1.call-update) | async-done | bytes 8388624 | tf_op jit(solution)/shard_map/all_gather | solution.py:40
  166.5 4.0 gather_fusion
  170.4 0.0 copy-done
  170.4 0.4 fusion.2
  170.8 0.4 fusion
  171.2 0.9 copy.11
  172.1 0.0 reduce-scatter.2.cloned.1.call-update
  172.1 0.0 all-reduce.2.cloned.1.call-start
  172.2 24.1 %reduce-scatter.2.cloned.1.call-done = f32[128,256]{1,0:T(8,128)} async-done(((f32[512,256]{1,0:T(8,128)}), f32[128,256]{1,0:T(8,128)}) %reduce-scatter.2.cloned.1.call-update) | async-done | bytes 131088 | tf_op jit(solution)/shard_map/reduce_scatter | solution.py:46
  196.3 1.8 convert_reduce_fusion
  198.2 1.8 fusion.8
  200.0 0.0 all-reduce.2.cloned.1.call-update
  200.0 96.6 %psum.15 = f32[256]{0:T(256)} all-reduce(f32[256]{0:T(256)S(1)} %get-tuple-element.3), channel_id=1, replica_groups=mesh['rows'=128,'rep'=4] {'rows','rep'}, use_global_device_ids=true, to_apply=%region_3.4 | all-reduce | flops 256 | bytes 2048 | tf_op jit(solution)/shard_map/psum | solution.py:58
  296.6 178.0 %all-reduce.2.cloned.1.call-done = f32[256,256]{1,0:T(8,128)} async-done(((f32[256,256]{1,0:T(8,128)}), f32[256,256]{1,0:T(8,128)}) %all-reduce.2.cloned.1.call-update) | async-done | bytes 262160 | tf_op jit(solution)/shard_map/psum | solution.py:58
  474.6 1.7 copy.16
  (1 shorter events, 0.0 us)
Async XLA Ops:
  7.2 163.3 %copy-start = (bf16[1,4,8,128,128]{4,3,2,1,0:T(8,128)(2,1)S(1)}, bf16[1,4,8,128,128]{4,3,2,1,0:T(8,128)(2,1)}, u32[]{:S(2)}) copy-start(bf16[1,4,8,128,128]{4,3,2,1,0:T(8,128)(2,1)} %param.11) | copy-start | bytes 3145732
  7.2 159.3 %all-gather.2.cloned.1.call-start = ((), (), s32[]{:S(2)}) async-start(), calls=%async_computation.1 | async-start | bytes 8454144 | tf_op jit(solution)/shard_map/all_gather | solution.py:40
  7.9 188.4 %reduce-scatter.2.cloned.1.call-start = ((), (), s32[]{:S(2)}) async-start(), calls=%async_computation.2 | async-start | bytes 655360 | tf_op jit(solution)/shard_map/reduce_scatter | solution.py:46
  172.1 302.5 %all-reduce.2.cloned.1.call-start = ((), (), s32[]{:S(2)}) async-start(), calls=%async_computation.3 | async-start | bytes 524288 | tf_op jit(solution)/shard_map/psum | solution.py:58
Sparse Core Ops, SparseCore 0:
  12.5 153.9 all-gather.1
  172.3 24.0 reduce-scatter.1
  201.9 272.6 all-reduce.1
where the time goes:
time: 483 us
  waiting for transfers between devices  357 us (74%)
  blocking collectives  96.6 us (20%)
  between operations  13.8 us (3%)
  local copies, waits for them, and re-layouts  8.46 us (2%)
    psum x1, waiting for transfers between devices, shards(): weight_grad, bias_grad = lax.psum((weight_term, bias_term), ('rows', 'rep'))  178 us
    all_gather x1, waiting for transfers between devices, shards(): stripe_nodes = lax.all_gather(features, 'rows', axis=0, tiled=True)  155 us
    psum x1, blocking collectives, shards(): weight_grad, bias_grad = lax.psum((weight_term, bias_term), ('rows', 'rep'))  96.6 us
    reduce_scatter x1, waiting for transfers between devices, shards(): lax.psum_scatter(partial_value, 'rep', scatter_dimension=0, tiled=True)  24.1 us
  transfers between devices with their start and end apart: 3, of which 3 were waited for; matrix products, arithmetic and copies ran while one was open for 1% of the time, Pallas kernels for 0%

commit v1 on v0

--- a/solution.py
+++ b/solution.py
@@ -37,7 +37,9 @@
     own_rows = lax.dynamic_slice_in_dim(tile_row[0], rep_index, 1, 0)
     own_cols = lax.dynamic_slice_in_dim(tile_col[0], rep_index, 1, 0)
     own_count = lax.dynamic_slice_in_dim(tile_count[0], rep_index, 1, 0)
-    stripe_nodes = lax.all_gather(features, "rows", axis=0, tiled=True)
+    stripe_nodes = jnp.concatenate(
+        lax.all_to_all(jnp.stack([features] * lax.axis_size("rows")), "rows", 0, 0), axis=0
+    )
     blocks = stripe_nodes.reshape(-1, block_size, feature_width)
     partial_value = propagate(
         own_tiles, own_rows, own_cols, own_count, blocks, row_count, slots_wide

time: 483 us -> 563 us (1.17)
  waiting for transfers between devices: 357 us -> 413 us
  starting transfers between devices: 0.12 us -> 20 us
    all_to_all x0 -> x1, waiting for transfers between devices: none -> 203 us  [shards(): lax.all_to_all(jnp.stack([features] * lax.axis_size('rows')), 'rows', 0, 0)]
    all_gather x1 -> x0, waiting for transfers between devices: 155 us -> none  [shards(): stripe_nodes = lax.all_gather(features, 'rows', axis=0, tiled=True)]
    all_to_all x0 -> x1, starting transfers between devices: none -> 19.9 us  [shards(): lax.all_to_all(jnp.stack([features] * lax.axis_size('rows')), 'rows', 0, 0)]
    reduce_scatter x1, waiting for transfers between devices: 24.1 us -> 32.6 us  [shards(): lax.psum_scatter(partial_value, 'rep', scatter_dimension=0, tiled=True)]
  transfers between devices with their start and end apart: 3 -> 3, of which waited for: 3 -> 3; matrix products, arithmetic and copies ran while one was open for 1% -> 0% of each run, Pallas kernels for 0% -> 0%
where the time goes in v1:
time: 563 us; the launch traced here: 562 us
  waiting for transfers between devices  413 us (73%)
  blocking collectives  97.2 us (17%)
  starting transfers between devices  20 us (4%)
  between operations  14.1 us (3%)
  local copies, waits for them, and re-layouts  13 us (2%)
    all_to_all x1, waiting for transfers between devices, shards(): lax.all_to_all(jnp.stack([features] * lax.axis_size('rows')), 'rows', 0, 0)  203 us
    psum x1, waiting for transfers between devices, shards(): weight_grad, bias_grad = lax.psum((weight_term, bias_term), ('rows', 'rep'))  177 us
    psum x1, blocking collectives, shards(): weight_grad, bias_grad = lax.psum((weight_term, bias_term), ('rows', 'rep'))  97.2 us
    reduce_scatter x1, waiting for transfers between devices, shards(): lax.psum_scatter(partial_value, 'rep', scatter_dimension=0, tiled=True)  32.6 us
    all_to_all x1, starting transfers between devices, shards(): lax.all_to_all(jnp.stack([features] * lax.axis_size('rows')), 'rows', 0, 0)  19.9 us
  transfers between devices with their start and end apart: 3, of which 3 were waited for; matrix products, arithmetic and copies ran while one was open for 0% of the time, Pallas kernels for 0%

profile of v1, /device:TPU:23, one launch (start us, length us, event | category | flops | bytes accessed | tf_op | source)
XLA Modules:
  0.0 562.5 jit_solution(6542214025020552814)
XLA Ops:
  7.2 0.0 copy-start
  7.2 5.2 stack.2
  12.4 0.0 copy-start.5
  12.4 0.0 copy-start.3
  12.4 0.0 copy-start.1
  12.4 0.0 copy-start.2
  12.4 0.0 copy-start.4
  12.4 19.9 %all-to-all-start = ((bf16[128,128,256]{2,1,0:T(8,128)(2,1)}), bf16[128,128,256]{2,1,0:T(8,128)(2,1)}, u32[]{:S(2)}, u32[]{:S(2)}) async-start(bf16[128,128,256]{2,1,0:T(8,128)(2,1)} %stack.2), calls=%async_computation | async-start | bytes 16777216 | tf_op jit(solution)/shard_map/all_to_all | solution.py:41
  32.3 0.0 reduce-scatter.2.cloned.1.call-start
  32.4 0.0 copy-done.5
  32.4 0.6 constant_dynamic-slice_fusion.1
  33.0 0.0 copy-done.3
  33.0 0.7 fusion.17
  33.7 0.6 iota_compare_fusion.1
  34.4 203.1 %all-to-all-done = bf16[128,128,256]{2,1,0:T(8,128)(2,1)} async-done(((bf16[128,128,256]{2,1,0:T(8,128)(2,1)}), bf16[128,128,256]{2,1,0:T(8,128)(2,1)}, u32[]{:S(2)}, u32[]{:S(2)}) %all-to-all-start) | async-done | bytes 8388640 | tf_op jit(solution)/shard_map/all_to_all | solution.py:41
  237.5 4.0 gather_fusion
  241.4 0.0 copy-done
  241.5 0.4 fusion.2
  241.8 0.4 fusion
  242.2 0.9 copy.11
  243.1 0.0 reduce-scatter.2.cloned.1.call-update
  243.1 0.0 all-reduce.2.cloned.1.call-start
  243.2 32.6 %reduce-scatter.2.cloned.1.call-done = f32[128,256]{1,0:T(8,128)} async-done(((f32[512,256]{1,0:T(8,128)}), f32[128,256]{1,0:T(8,128)}) %reduce-scatter.2.cloned.1.call-update) | async-done | bytes 131088 | tf_op jit(solution)/shard_map/reduce_scatter | solution.py:48
  275.8 0.0 copy-done.1
  275.8 0.0 copy-done.2
  275.8 0.0 copy-done.4
  275.8 1.8 convert_reduce_fusion
  277.6 1.8 fusion.8
  279.4 0.0 all-reduce.2.cloned.1.call-update
  279.4 97.2 %psum.15 = f32[256]{0:T(256)} all-reduce(f32[256]{0:T(256)S(1)} %get-tuple-element.3), channel_id=1, replica_groups=mesh['rows'=128,'rep'=4] {'rows','rep'}, use_global_device_ids=true, to_apply=%region_3.4 | all-reduce | flops 256 | bytes 2048 | tf_op jit(solution)/shard_map/psum | solution.py:60
  376.6 177.3 %all-reduce.2.cloned.1.call-done = f32[256,256]{1,0:T(8,128)} async-done(((f32[256,256]{1,0:T(8,128)}), f32[256,256]{1,0:T(8,128)}) %all-reduce.2.cloned.1.call-update) | async-done | bytes 262160 | tf_op jit(solution)/shard_map/psum | solution.py:60
  554.0 1.7 copy.16
  (3 shorter events, 0.0 us)
Async XLA Ops:
  7.2 234.3 %copy-start = (bf16[1,4,8,128,128]{4,3,2,1,0:T(8,128)(2,1)S(1)}, bf16[1,4,8,128,128]{4,3,2,1,0:T(8,128)(2,1)}, u32[]{:S(2)}) copy-start(bf16[1,4,8,128,128]{4,3,2,1,0:T(8,128)(2,1)} %param.11) | copy-start | bytes 3145732
  12.4 20.0 %copy-start.5 = (s32[1,4]{1,0:T(1,128)S(1)}, s32[1,4]{1,0:T(1,128)}, u32[]{:S(2)}) copy-start(s32[1,4]{1,0:T(1,128)} %param.14) | copy-start | bytes 52
  12.4 20.6 %copy-start.3 = (s32[1,4,8]{2,1,0:T(4,128)S(1)}, s32[1,4,8]{2,1,0:T(4,128)}, u32[]{:S(2)}) copy-start(s32[1,4,8]{2,1,0:T(4,128)} %param.13) | copy-start | bytes 388
  12.4 263.4 %copy-start.1 = (bf16[256,256]{1,0:T(8,128)(2,1)S(1)}, bf16[256,256]{1,0:T(8,128)(2,1)}, u32[]{:S(2)}) copy-start(bf16[256,256]{1,0:T(8,128)(2,1)} %param.9) | copy-start | bytes 393220
  12.4 263.4 %copy-start.2 = (bf16[128,256]{1,0:T(8,128)(2,1)S(1)}, bf16[128,256]{1,0:T(8,128)(2,1)}, u32[]{:S(2)}) copy-start(bf16[128,256]{1,0:T(8,128)(2,1)} %param.15) | copy-start | bytes 196612
  12.4 263.4 %copy-start.4 = (f32[256]{0:T(256)S(1)}, f32[256]{0:T(256)}, u32[]{:S(2)}) copy-start(f32[256]{0:T(256)} %param.10) | copy-start | bytes 3076
  12.4 225.1 %all-to-all-start = ((bf16[128,128,256]{2,1,0:T(8,128)(2,1)}), bf16[128,128,256]{2,1,0:T(8,128)(2,1)}, u32[]{:S(2)}, u32[]{:S(2)}) async-start(bf16[128,128,256]{2,1,0:T(8,128)(2,1)} %stack.2), calls=%async_computation | async-start | bytes 16777216 | tf_op jit(solution)/shard_map/all_to_all | solution.py:41
  32.3 243.5 %reduce-scatter.2.cloned.1.call-start = ((), (), s32[]{:S(2)}) async-start(), calls=%async_computation.2 | async-start | bytes 655360 | tf_op jit(solution)/shard_map/reduce_scatter | solution.py:48
  243.1 310.8 %all-reduce.2.cloned.1.call-start = ((), (), s32[]{:S(2)}) async-start(), calls=%async_computation.3 | async-start | bytes 524288 | tf_op jit(solution)/shard_map/psum | solution.py:60
Sparse Core Ops, SparseCore 0:
  243.3 32.4 reduce-scatter.1
  281.3 272.5 all-reduce.1
